TPU v7x, 256 devices: a whole 4x4x8 slice. The times are simulated.
256 devices in a mesh: dp: 8 (over y, core), expert: 32 (over z, x).
Axes of the slice: x: 4, y: 4, z: 8, core: 2. Of those that a mesh axis runs over, the one named last changes fastest.
Arguments:
- tokens: bfloat16 [4096, 4096], P('expert', 'dp'), may hold values from -6 to 6
- expert_ids: int32 [4096, 8], P('expert'), may hold values from 0 to 63, all different within a row; in each aligned block of 128 rows (0 to 127, 128 to 255, ...) at most 24 rows name the same one
- route_weights: float32 [4096, 8], P('expert'), may hold values from 0.1 to 0.4
- gate_up_weight: bfloat16 [64, 4096, 1536], P('expert', 'dp'), may hold values from -0.09375 to 0.09375
- down_weight: bfloat16 [64, 768, 4096], P('expert', None, 'dp'), may hold values from -0.21875 to 0.21875
- out_grad: bfloat16 [4096, 4096], P('expert', 'dp'), may hold values from -6 to 6
Outputs:
- layer_out: bfloat16 [4096, 4096], P('expert', 'dp')
- token_grad: bfloat16 [4096, 4096], P('expert', 'dp')
- route_grad: float32 [4096, 8], P('expert')
- gate_up_grad: bfloat16 [64, 4096, 1536], P('expert', 'dp')
- down_grad: bfloat16 [64, 768, 4096], P('expert', None, 'dp')
Inputs may be any that keep to these rules, and one draw needn't show every extreme that they name: `expert_ids`: each row names 8 different experts. Among the 128 rows of one group no expert is named more than 24 times, and in every draw some group names some expert exactly 24 times.
All inputs are finite; a program needn't handle non-finite values.
Results may differ from a plain program's by a relative error of at most 0.029.
Values may be sent and summed in bfloat16 or wider, within the bound.
No kernel may reach another device: no remote copies, remote signals or barrier semaphores. Data moves between devices by JAX's collectives and lax.ppermute only.
A program may use at most 128 MiB of HBM per device.

v0:
```python
import jax
import jax.numpy as jnp
from jax import lax
from jax.sharding import PartitionSpec as P


def local(tokens, expert_ids, route_weights, gate_up_weight, down_weight, out_grad):
    tok_count, piece_width = tokens.shape
    top_count = expert_ids.shape[1]
    group_count = lax.axis_size("expert")
    local_count = gate_up_weight.shape[0]
    hidden_units = down_weight.shape[1]
    expert_total = local_count * group_count
    capacity = 3 * tok_count * top_count // (2 * expert_total)
    slot_count = expert_total * capacity
    rows_all = group_count * capacity
    route_count = tok_count * top_count
    block_shape = (local_count, group_count, capacity, piece_width)
    route_ids = expert_ids.reshape(-1)
    onehot = (route_ids[:, None] == jnp.arange(expert_total, dtype=jnp.int32)[None, :]).astype(
        jnp.int32
    )
    slot_rank = jnp.sum(onehot * (jnp.cumsum(onehot, axis=0) - 1), axis=1)
    slot_index = (
        route_ids % local_count * rows_all + route_ids // local_count * capacity + slot_rank
    )
    slot_route = (
        jnp.full((slot_count,), route_count, jnp.int32)
        .at[slot_index]
        .set(jnp.arange(route_count, dtype=jnp.int32))
    )
    source_tok = slot_route // top_count
    weight_flat = route_weights.reshape(-1)
    weight_padded = jnp.concatenate([weight_flat, jnp.zeros((1,), jnp.float32)], axis=0)
    tokens_padded = jnp.concatenate([tokens, jnp.zeros((1, piece_width), tokens.dtype)], axis=0)
    grad_padded = jnp.concatenate([out_grad, jnp.zeros((1, piece_width), out_grad.dtype)], axis=0)
    outbound = tokens_padded[source_tok]
    grad_outbound = (
        weight_padded[slot_route][:, None] * grad_padded[source_tok].astype(jnp.float32)
    ).astype(jnp.bfloat16)
    arrived, grad_arrived = (
        lax.all_to_all(
            outbound.reshape(block_shape), "expert", split_axis=1, concat_axis=1, tiled=True
        ),
        lax.all_to_all(
            grad_outbound.reshape(block_shape), "expert", split_axis=1, concat_axis=1, tiled=True
        ),
    )
    arrived = arrived.reshape(local_count, rows_all, piece_width)
    grad_arrived = grad_arrived.reshape(local_count, rows_all, piece_width)
    rows = arrived
    preact = lax.psum_scatter(
        jnp.einsum("lrk,lkf->rlf", rows, gate_up_weight, preferred_element_type=jnp.float32).astype(
            jnp.bfloat16
        ),
        "dp",
        scatter_dimension=0,
        tiled=True,
    ).astype(jnp.float32)
    gate_pre = preact[..., :hidden_units]
    up_pre = preact[..., hidden_units:]
    sigmoid_gate = jax.nn.sigmoid(gate_pre)
    activation = gate_pre * sigmoid_gate
    hidden_mine = (activation * up_pre).astype(jnp.bfloat16)
    hidden_all = lax.all_gather(hidden_mine, "dp", axis=0, tiled=True)
    out_slice = jnp.einsum(
        "rlf,lfk->lrk", hidden_all, down_weight, preferred_element_type=jnp.float32
    ).astype(jnp.bfloat16)
    grad_routes = jnp.repeat(out_grad, top_count, axis=0).astype(jnp.float32)
    returned = lax.all_to_all(
        out_slice.reshape(block_shape), "expert", split_axis=1, concat_axis=1, tiled=True
    )
    y_routes = returned.reshape(slot_count, piece_width)[slot_index].astype(jnp.float32)
    layer_out = (
        (weight_flat[:, None] * y_routes)
        .reshape(tok_count, top_count, piece_width)
        .sum(axis=1)
        .astype(jnp.bfloat16)
    )
    partial_dot = jnp.sum(grad_routes * y_routes, axis=1).reshape(tok_count, top_count)
    route_grad = lax.psum(partial_dot, "dp")
    layer_out, route_grad = (layer_out, route_grad)
    rows = grad_arrived
    hidden_grad = lax.psum_scatter(
        jnp.einsum("lrk,lfk->rlf", rows, down_weight, preferred_element_type=jnp.float32).astype(
            jnp.bfloat16
        ),
        "dp",
        scatter_dimension=0,
        tiled=True,
    ).astype(jnp.float32)
    gate_grad = hidden_grad * up_pre * sigmoid_gate * (1.0 + gate_pre * (1.0 - sigmoid_gate))
    up_grad = hidden_grad * activation
    preact_grad = jnp.concatenate([gate_grad, up_grad], axis=2).astype(jnp.bfloat16)
    preact_grad_all = lax.all_gather(preact_grad, "dp", axis=0, tiled=True)
    x_grad_slice = jnp.einsum(
        "rlf,lkf->lrk", preact_grad_all, gate_up_weight, preferred_element_type=jnp.float32
    ).astype(jnp.bfloat16)
    gate_up_grad = jnp.einsum(
        "lrk,rlf->lkf", arrived, preact_grad_all, preferred_element_type=jnp.float32
    ).astype(jnp.bfloat16)
    down_grad = jnp.einsum(
        "rlf,lrk->lfk", hidden_all, grad_arrived, preferred_element_type=jnp.float32
    ).astype(jnp.bfloat16)
    grad_back = lax.all_to_all(
        x_grad_slice.reshape(block_shape), "expert", split_axis=1, concat_axis=1, tiled=True
    )
    grad_per_route = grad_back.reshape(slot_count, piece_width)[slot_index].astype(jnp.float32)
    token_grad = (
        grad_per_route.reshape(tok_count, top_count, piece_width).sum(axis=1).astype(jnp.bfloat16)
    )
    return (layer_out, token_grad, route_grad, gate_up_grad, down_grad)


def solution(mesh):
    placed = (
        P("expert", "dp"),
        P("expert", None),
        P("expert", None),
        P("expert", "dp", None),
        P("expert", None, "dp"),
        P("expert", "dp"),
    )
    return jax.shard_map(
        local,
        mesh=mesh,
        in_specs=placed,
        out_specs=(
            P("expert", "dp"),
            P("expert", "dp"),
            P("expert", None),
            P("expert", "dp", None),
            P("expert", None, "dp"),
        ),
        check_vma=False,
    )
```

profile of v0, /device:TPU:2, one launch (start us, length us, event | category | flops | bytes accessed | tf_op | source)
XLA Modules:
  0.0 371.5 jit_solution(12130872056310802385)
XLA Ops:
  7.2 0.0 reduce-scatter.3.cloned.1.call-start
  7.2 0.9 copy.23
  8.2 0.1 eq.31
  8.3 0.1 eq.27
  8.3 0.1 reshape.210
  8.4 0.7 fusion.11
  9.2 31.1 %reduce-window.6 = s32[64,8,128]{2,1,0:T(8,128)S(1)} reduce-window(s32[64,8,128]{2,1,0:T(8,128)} %fusion.11, s32[]{:T(128)} %constant.55.clone.1), window={size=1x1x128 pad=0_0x0_0x127_0}, to_apply=%region_0.0 | reduce-window | flops 8323072 | bytes 524292 | tf_op jit(solution)/shard_map/reduce-window
  40.3 0.8 slice.26
  41.1 1.1 copy.26
  42.2 0.1 copy.27
  42.3 0.1 add_add_fusion
  42.5 0.1 fusion.10
  42.6 4.3 %scatter_custom_fusion = s32[1536]{0:T(1024)S(1)} fusion(s32[1024]{0:T(1024)S(1)} %bitcast.64, s32[1024]{0:T(1024)S(1)} %iota.11, s32[]{:T(128)} %constant.54.clone.1), kind=kCustom, calls=%fused_computation.58 | custom fusion | bytes 6148 | tf_op jit(solution)/shard_map/scatter | solution.py:30
  46.9 0.9 concatenate.13
  47.9 5.4 %gather_fusion = bf16[1536,512]{1,0:T(8,128)(2,1)} fusion(bf16[129,512]{1,0:T(8,128)(2,1)S(1)} %concatenate.13, s32[2048]{0:T(1024)S(1)} %get-tuple-element.21), kind=kCustom, calls=%fused_computation | custom fusion | bytes 3151872 | tf_op jit(solution)/shard_map/gather | solution.py:37
  53.3 1.6 copy.28
  54.9 50.7 %all_to_all.20 = bf16[2,32,24,512]{3,2,0,1:T(8,128)(2,1)S(1)} all-to-all(bf16[2,32,24,512]{3,2,0,1:T(8,128)(2,1)S(1)} %copy.28), channel_id=1, replica_groups=mesh['dp'=8,'expert'=32] {'expert'}, dimensions={1} | all-to-all | bytes 3145728 | tf_op jit(solution)/shard_map/all_to_all | solution.py:42
  105.6 0.1 copy.29
  105.7 1.2 copy-done.1
  106.9 4.2 %convert_bitcast_fusion = bf16[768,2,1536]{2,0,1:T(8,128)(2,1)} fusion(bf16[2,768,512]{2,1,0:T(8,128)(2,1)S(1)} %bitcast.55, bf16[2,512,1536]{2,1,0:T(8,128)(2,1)S(1)} %copy-done), kind=kOutput, calls=%fused_computation.6 | convolution fusion | flops 2418278400 | bytes 9437184 | tf_op jit(solution)/shard_map/lrk,lkf->rlf/dot_general | solution.py:53
  111.1 0.0 reduce-scatter.5.cloned.1.call-start
  111.1 0.8 copy-done.3
  112.0 5.4 %gather_fusion.3 = bf16[1536,512]{1,0:T(8,128)(2,1)} fusion(bf16[129,512]{1,0:T(8,128)(2,1)S(1)} %concatenate.15, s32[2048]{0:T(1024)S(1)} %get-tuple-element.21), kind=kCustom, calls=%fused_computation.3 | custom fusion | bytes 3151872 | tf_op jit(solution)/shard_map/gather | solution.py:39
  117.4 0.1 copy.22
  117.5 0.1 reshape.216
  117.6 8.4 %gather_fusion.2 = f32[1536]{0:T(1024)S(1)} fusion(f32[1025]{0:T(1024)S(1)} %pad_maximum_fusion.1, s32[2048]{0:T(1024)S(1)} %get-tuple-element.20), kind=kCustom, calls=%fused_computation.2 | custom fusion | bytes 18432 | tf_op jit(solution)/shard_map/gather | solution.py:39
  126.0 0.1 mul.86
  126.1 1.8 fusion
  128.0 43.9 %all_to_all.21 = bf16[2,32,24,512]{3,2,0,1:T(8,128)(2,1)S(1)} all-to-all(bf16[2,32,24,512]{3,2,0,1:T(8,128)(2,1)S(1)} %fusion), channel_id=1, replica_groups=mesh['dp'=8,'expert'=32] {'expert'}, dimensions={1} | all-to-all | bytes 3145728 | tf_op jit(solution)/shard_map/all_to_all | solution.py:45
  171.8 0.1 copy.35
  172.0 1.2 copy-done.2
  173.2 0.6 copy-done.5
  173.8 2.8 convert_bitcast_fusion.2
  176.6 0.0 reduce-scatter.5.cloned.1.call-update
  176.7 0.0 all-gather.3.cloned.1.call-start
  176.7 0.0 reduce-scatter.3.cloned.1.call-done
  176.7 2.2 convert_element_type.77
  178.9 31.8 %reduce-scatter.5.cloned.1.call-done = bf16[96,2,768]{2,0,1:T(8,128)(2,1)} async-done(((bf16[768,2,768]{2,0,1:T(8,128)(2,1)}), bf16[96,2,768]{2,0,1:T(8,128)(2,1)}) %reduce-scatter.5.cloned.1.call-update) | async-done | bytes 294928 | tf_op jit(solution)/shard_map/reduce_scatter | solution.py:84
  210.7 2.5 fusion.6
  213.2 0.0 all-gather.3.cloned.1.call-update
  213.3 0.0 all-gather.5.cloned.1.call-start
  213.3 1.8 pad_maximum_fusion
  215.2 25.3 %all-gather.3.cloned.1.call-done = bf16[768,2,768]{2,0,1:T(8,128)(2,1)} async-done(((bf16[96,2,768]{2,0,1:T(8,128)(2,1)}), bf16[768,2,768]{2,0,1:T(8,128)(2,1)}) %all-gather.3.cloned.1.call-update) | async-done | bytes 2359312 | tf_op jit(solution)/shard_map/all_gather | solution.py:65
  240.4 3.5 convolution_convert_fusion.2
  243.9 1.4 copy.30
  245.3 10.2 %all-to-all-start.1 = ((bf16[2,32,24,512]{3,2,0,1:T(8,128)(2,1)}), bf16[2,32,24,512]{3,2,0,1:T(8,128)(2,1)}, u32[]{:S(2)}, u32[]{:S(2)}) async-start(bf16[2,32,24,512]{3,2,0,1:T(8,128)(2,1)} %copy.30), calls=%async_computation.2 | async-start | bytes 3145728 | tf_op jit(solution)/shard_map/all_to_all | solution.py:70
  255.5 24.6 %all-gather.5.cloned.1.call-done = bf16[768,2,1536]{2,0,1:T(8,128)(2,1)} async-done(((bf16[96,2,1536]{2,0,1:T(8,128)(2,1)}), bf16[768,2,1536]{2,0,1:T(8,128)(2,1)}) %all-gather.5.cloned.1.call-update) | async-done | bytes 4718608 | tf_op jit(solution)/shard_map/all_gather | solution.py:95
  280.1 5.0 %convolution_convert_fusion.3 = bf16[2,768,512]{2,1,0:T(8,128)(2,1)S(1)} fusion(bf16[768,2,1536]{2,0,1:T(8,128)(2,1)} %all-gather.5.cloned.1.call-done, bf16[2,512,1536]{2,1,0:T(8,128)(2,1)S(1)} %copy-done), kind=kOutput, calls=%fused_computation.18 | convolution fusion | flops 2416705536 | bytes 9437184 | tf_op jit(solution)/shard_map/rlf,lkf->lrk/dot_general | solution.py:96
  285.1 1.5 copy.36
  286.5 7.8 %all-to-all-done.1 = bf16[2,32,24,512]{3,2,0,1:T(8,128)(2,1)} async-done(((bf16[2,32,24,512]{3,2,0,1:T(8,128)(2,1)}), bf16[2,32,24,512]{3,2,0,1:T(8,128)(2,1)}, u32[]{:S(2)}, u32[]{:S(2)}) %all-to-all-start.1) | async-done | bytes 1572896 | tf_op jit(solution)/shard_map/all_to_all | solution.py:70
  294.3 6.6 %all-to-all-start.3 = ((bf16[2,32,24,512]{3,2,0,1:T(8,128)(2,1)}), bf16[2,32,24,512]{3,2,0,1:T(8,128)(2,1)}, u32[]{:S(2)}, u32[]{:S(2)}) async-start(bf16[2,32,24,512]{3,2,0,1:T(8,128)(2,1)} %copy.36), calls=%async_computation.5 | async-start | bytes 3145728 | tf_op jit(solution)/shard_map/all_to_all | solution.py:105
  300.9 0.9 convert_element_type.90
  301.8 4.7 %convolution_convert_fusion.1 = bf16[2,768,512]{2,1,0:T(8,128)(2,1)} fusion(bf16[768,2,768]{2,0,1:T(8,128)(2,1)} %all-gather.3.cloned.1.call-done, bf16[2,768,512]{2,1,0:T(8,128)(2,1)} %bitcast.58), kind=kOutput, calls=%fused_computation.16 | convolution fusion | flops 1208745984 | bytes 5505024 | tf_op jit(solution)/shard_map/rlf,lrk->lfk/dot_general | solution.py:102
  306.5 2.7 copy.31
  309.2 6.7 %gather_fusion.1 = bf16[1024,512]{1,0:T(8,128)(2,1)} fusion(bf16[1536,512]{1,0:T(8,128)(2,1)} %bitcast.52, s32[1024]{0:T(1024)S(1)} %broadcast_clamp_fusion), kind=kCustom, calls=%fused_computation.1 | custom fusion | bytes 2101248 | tf_op jit(solution)/shard_map/gather | solution.py:73
  315.9 1.5 fusion.3
  317.4 0.1 reduce_sum.48
  317.5 25.1 %psum.7 = f32[128,8]{1,0:T(8,128)S(1)} all-reduce(f32[128,8]{1,0:T(8,128)S(1)} %reduce_sum.48), channel_id=1, replica_groups=mesh['dp'=8,'expert'=32] {'dp'}, use_global_device_ids=true, to_apply=%region_9.10 | all-reduce | flops 1024 | bytes 8192 | tf_op jit(solution)/shard_map/psum | solution.py:81
  342.6 0.7 copy.39
  343.3 2.6 fusion.2
  345.9 7.1 %convolution_convert_fusion = bf16[2,512,1536]{2,1,0:T(8,128)(2,1)} fusion(bf16[2,768,512]{2,1,0:T(8,128)(2,1)} %bitcast.56, bf16[768,2,1536]{2,0,1:T(8,128)(2,1)} %all-gather.5.cloned.1.call-done), kind=kOutput, calls=%fused_computation.7 | convolution fusion | flops 2417491968 | bytes 9437184 | tf_op jit(solution)/shard_map/lrk,rlf->lkf/dot_general | solution.py:99
  353.0 2.7 copy.37
  355.7 6.7 %gather_fusion.4 = bf16[1024,512]{1,0:T(8,128)(2,1)} fusion(bf16[1536,512]{1,0:T(8,128)(2,1)} %bitcast.51, s32[1024]{0:T(1024)S(1)} %broadcast_clamp_fusion), kind=kCustom, calls=%fused_computation.4 | custom fusion | bytes 2101248 | tf_op jit(solution)/shard_map/gather | solution.py:108
  362.4 2.6 bitcast_reduce_fusion
  (21 shorter events, 0.2 us)
Async XLA Ops:
  7.2 99.7 %copy-start = (bf16[2,512,1536]{2,1,0:T(8,128)(2,1)S(1)}, bf16[2,512,1536]{2,1,0:T(8,128)(2,1)}, u32[]{:S(2)}) copy-start(bf16[2,512,1536]{2,1,0:T(8,128)(2,1)} %param.9) | copy-start | bytes 9437188
  7.2 169.5 %reduce-scatter.3.cloned.1.call-start = ((), (), s32[]{:S(2)}) async-start(), calls=%async_computation.6 | async-start | bytes 5308416 | tf_op jit(solution)/shard_map/reduce_scatter | solution.py:52
  105.7 1.2 copy-start.1
  111.1 0.9 copy-start.3
  111.1 99.6 %reduce-scatter.5.cloned.1.call-start = ((), (), s32[]{:S(2)}) async-start(), calls=%async_computation.8 | async-start | bytes 2654208 | tf_op jit(solution)/shard_map/reduce_scatter | solution.py:84
  112.0 5.4 %copy-start.4 = (f32[128,8]{0,1:T(8,128)S(1)}, f32[128,8]{0,1:T(8,128)}, u32[]{:S(2)}) copy-start(f32[128,8]{0,1:T(8,128)} %param.8) | copy-start | bytes 12292
  171.8 2.0 copy-start.5
  172.0 1.2 copy-start.2
  176.7 63.8 %all-gather.3.cloned.1.call-start = ((), (), s32[]{:S(2)}) async-start(), calls=%async_computation.7 | async-start | bytes 2654208 | tf_op jit(solution)/shard_map/all_gather | solution.py:65
  213.3 66.8 %all-gather.5.cloned.1.call-start = ((), (), s32[]{:S(2)}) async-start(), calls=%async_computation.9 | async-start | bytes 5308416 | tf_op jit(solution)/shard_map/all_gather | solution.py:95
  245.3 49.0 %all-to-all-start.1 = ((bf16[2,32,24,512]{3,2,0,1:T(8,128)(2,1)}), bf16[2,32,24,512]{3,2,0,1:T(8,128)(2,1)}, u32[]{:S(2)}, u32[]{:S(2)}) async-start(bf16[2,32,24,512]{3,2,0,1:T(8,128)(2,1)} %copy.30), calls=%async_computation.2 | async-start | bytes 3145728 | tf_op jit(solution)/shard_map/all_to_all | solution.py:70
  294.3 58.7 %all-to-all-start.3 = ((bf16[2,32,24,512]{3,2,0,1:T(8,128)(2,1)}), bf16[2,32,24,512]{3,2,0,1:T(8,128)(2,1)}, u32[]{:S(2)}, u32[]{:S(2)}) async-start(bf16[2,32,24,512]{3,2,0,1:T(8,128)(2,1)} %copy.36), calls=%async_computation.5 | async-start | bytes 3145728 | tf_op jit(solution)/shard_map/all_to_all | solution.py:105
Sparse Core Ops, SparseCore 0:
  111.2 38.6 reduce-scatter.2
  176.8 33.9 reduce-scatter.4
  213.4 26.9 all-gather.2
  242.7 37.3 all-gather.4
where the time goes:
time: 374 us; the launch traced here: 372 us
  blocking collectives  120 us (32%)
  waiting for transfers between devices  89.5 us (24%)
  local copies, waits for them, and re-layouts  56 us (15%)
  other arithmetic  48.1 us (13%)
  matrix products  27.3 us (7%)
  starting transfers between devices  16.9 us (5%)
  between operations  14 us (4%)
    all_to_all x1, blocking collectives, local(): lax.all_to_all(outbound.reshape(block_shape), 'expert', split_axis=1, con...  50.7 us
    all_to_all x1, blocking collectives, local(): lax.all_to_all(grad_outbound.reshape(block_shape), 'expert', split_axis=1...  43.9 us
    another operation x3, other arithmetic  33.6 us
    reduce_scatter x1, waiting for transfers between devices, local(): lax.psum_scatter(jnp.einsum('lrk,lfk->rlf', rows, down_weight, preferred_...  31.8 us
    all_gather x1, waiting for transfers between devices, local(): hidden_all = lax.all_gather(hidden_mine, 'dp', axis=0, tiled=True)  25.3 us
    psum x1, blocking collectives, local(): route_grad = lax.psum(partial_dot, 'dp')  25.1 us
    all_gather x1, waiting for transfers between devices, local(): preact_grad_all = lax.all_gather(preact_grad, 'dp', axis=0, tiled=True)  24.6 us
    all_to_all x1, starting transfers between devices, local(): lax.all_to_all(out_slice.reshape(block_shape), 'expert', split_axis=1, co...  10.2 us
  transfers between devices with their start and end apart: 6, of which 4 were waited for; matrix products, arithmetic and copies ran while one was open for 16% of the time, Pallas kernels for 0%

commit v1 on v0

--- a/solution.py
+++ b/solution.py
@@ -18,36 +18,34 @@
     block_shape = (local_count, group_count, capacity, piece_width)
     route_ids = expert_ids.reshape(-1)
     onehot = (route_ids[:, None] == jnp.arange(expert_total, dtype=jnp.int32)[None, :]).astype(
-        jnp.int32
+        jnp.bfloat16
     )
-    slot_rank = jnp.sum(onehot * (jnp.cumsum(onehot, axis=0) - 1), axis=1)
+    order = jnp.arange(route_count, dtype=jnp.int32)
+    lower = (order[None, :] < order[:, None]).astype(jnp.bfloat16)
+    earlier = jnp.dot(lower, onehot, preferred_element_type=jnp.float32)
+    slot_rank = jnp.sum(onehot.astype(jnp.float32) * earlier, axis=1).astype(jnp.int32)
     slot_index = (
         route_ids % local_count * rows_all + route_ids // local_count * capacity + slot_rank
     )
-    slot_route = (
-        jnp.full((slot_count,), route_count, jnp.int32)
-        .at[slot_index]
-        .set(jnp.arange(route_count, dtype=jnp.int32))
+    route_hit = slot_index[:, None] == jnp.arange(slot_count, dtype=jnp.int32)[None, :]
+    token_hit = jnp.any(route_hit.reshape(tok_count, top_count, slot_count), axis=1).astype(
+        jnp.bfloat16
     )
-    source_tok = slot_route // top_count
     weight_flat = route_weights.reshape(-1)
-    weight_padded = jnp.concatenate([weight_flat, jnp.zeros((1,), jnp.float32)], axis=0)
-    tokens_padded = jnp.concatenate([tokens, jnp.zeros((1, piece_width), tokens.dtype)], axis=0)
-    grad_padded = jnp.concatenate([out_grad, jnp.zeros((1, piece_width), out_grad.dtype)], axis=0)
-    outbound = tokens_padded[source_tok]
+    slot_weight = jnp.sum(jnp.where(route_hit, weight_flat[:, None], 0.0), axis=0)
+    outbound = lax.dot_general(
+        token_hit, tokens, (((0,), (0,)), ((), ())), preferred_element_type=jnp.float32
+    ).astype(jnp.bfloat16)
     grad_outbound = (
-        weight_padded[slot_route][:, None] * grad_padded[source_tok].astype(jnp.float32)
+        slot_weight[:, None]
+        * lax.dot_general(
+            token_hit, out_grad, (((0,), (0,)), ((), ())), preferred_element_type=jnp.float32
+        )
     ).astype(jnp.bfloat16)
-    arrived, grad_arrived = (
-        lax.all_to_all(
-            outbound.reshape(block_shape), "expert", split_axis=1, concat_axis=1, tiled=True
-        ),
-        lax.all_to_all(
-            grad_outbound.reshape(block_shape), "expert", split_axis=1, concat_axis=1, tiled=True
-        ),
-    )
-    arrived = arrived.reshape(local_count, rows_all, piece_width)
-    grad_arrived = grad_arrived.reshape(local_count, rows_all, piece_width)
+    both = jnp.stack([outbound, grad_outbound]).reshape((2,) + block_shape)
+    both = lax.all_to_all(both, "expert", split_axis=2, concat_axis=2, tiled=True)
+    arrived = both[0].reshape(local_count, rows_all, piece_width)
+    grad_arrived = both[1].reshape(local_count, rows_all, piece_width)
     rows = arrived
     preact = lax.psum_scatter(
         jnp.einsum("lrk,lkf->rlf", rows, gate_up_weight, preferred_element_type=jnp.float32).astype(
@@ -70,7 +68,10 @@
     returned = lax.all_to_all(
         out_slice.reshape(block_shape), "expert", split_axis=1, concat_axis=1, tiled=True
     )
-    y_routes = returned.reshape(slot_count, piece_width)[slot_index].astype(jnp.float32)
+    route_pick = route_hit.astype(jnp.bfloat16)
+    y_routes = jnp.dot(
+        route_pick, returned.reshape(slot_count, piece_width), preferred_element_type=jnp.float32
+    )
     layer_out = (
         (weight_flat[:, None] * y_routes)
         .reshape(tok_count, top_count, piece_width)
@@ -79,7 +80,6 @@
     )
     partial_dot = jnp.sum(grad_routes * y_routes, axis=1).reshape(tok_count, top_count)
     route_grad = lax.psum(partial_dot, "dp")
-    layer_out, route_grad = (layer_out, route_grad)
     rows = grad_arrived
     hidden_grad = lax.psum_scatter(
         jnp.einsum("lrk,lfk->rlf", rows, down_weight, preferred_element_type=jnp.float32).astype(
@@ -105,10 +105,9 @@
     grad_back = lax.all_to_all(
         x_grad_slice.reshape(block_shape), "expert", split_axis=1, concat_axis=1, tiled=True
     )
-    grad_per_route = grad_back.reshape(slot_count, piece_width)[slot_index].astype(jnp.float32)
-    token_grad = (
-        grad_per_route.reshape(tok_count, top_count, piece_width).sum(axis=1).astype(jnp.bfloat16)
-    )
+    token_grad = jnp.dot(
+        token_hit, grad_back.reshape(slot_count, piece_width), preferred_element_type=jnp.float32
+    ).astype(jnp.bfloat16)
     return (layer_out, token_grad, route_grad, gate_up_grad, down_grad)
 
 

time: 374 us -> 329 us (0.88)
  local copies, waits for them, and re-layouts: 56 us -> 14.6 us
  waiting for transfers between devices: 89.5 us -> 128 us
  other arithmetic: 48.1 us -> 11.4 us
  blocking collectives: 120 us -> 110 us
  matrix products: 27.3 us -> 34 us
    reduce_scatter x1, waiting for transfers between devices: 0.02 us -> 32.9 us  [local(): lax.psum_scatter(jnp.einsum('lrk,lkf->rlf', rows, gate_up_weight, preferr...]
    gather x5 -> x0, local copies, waits for them, and re-layouts: 32.6 us -> none  [the longest x1 8.39 us: local(): weight_padded[slot_route][:, None]]
    another operation x3 -> x2, other arithmetic: 33.6 us -> 2.9 us
    all_to_all x2 -> x1, blocking collectives: 94.6 us -> 84.4 us  [local(): lax.all_to_all(both, 'expert', split_axis=2, concat_axis=2, tiled=True)]
    dot_general x0 -> x5, matrix products: none -> 6.69 us  [the longest x1 2.9 us: local(): jnp.dot(route_pick, returned.reshape(slot_count, piece_width), preferred_...]
    reduce_scatter x1, waiting for transfers between devices: 31.8 us -> 37.1 us  [local(): lax.psum_scatter(jnp.einsum('lrk,lfk->rlf', rows, down_weight, preferred_...]
    reduce_sum x3 -> x1, other arithmetic: 5.24 us -> 0.83 us  [local(): jnp.sum(jnp.where(route_hit, weight_flat[:, None], 0.0), axis=0)]
    scatter x1 -> x0, local copies, waits for them, and re-layouts: 4.32 us -> none  [local(): slot_route = jnp.full((slot_count,), route_count, jnp.int32).at[slot_inde...]
  transfers between devices with their start and end apart: 6 -> 6, of which waited for: 4 -> 5; matrix products, arithmetic and copies ran while one was open for 16% -> 11% of each run, Pallas kernels for 0% -> 0%
where the time goes in v1:
time: 329 us; the launch traced here: 328 us
  waiting for transfers between devices  128 us (39%)
  blocking collectives  110 us (33%)
  matrix products  34 us (10%)
  starting transfers between devices  16.9 us (5%)
  local copies, waits for them, and re-layouts  14.6 us (4%)
  between operations  14 us (4%)
  other arithmetic  11.4 us (3%)
    all_to_all x1, blocking collectives, local(): lax.all_to_all(both, 'expert', split_axis=2, concat_axis=2, tiled=True)  84.4 us
    reduce_scatter x1, waiting for transfers between devices, local(): lax.psum_scatter(jnp.einsum('lrk,lfk->rlf', rows, down_weight, preferred_...  37.1 us
    reduce_scatter x1, waiting for transfers between devices, local(): lax.psum_scatter(jnp.einsum('lrk,lkf->rlf', rows, gate_up_weight, preferr...  32.9 us
    all_gather x1, waiting for transfers between devices, local(): hidden_all = lax.all_gather(hidden_mine, 'dp', axis=0, tiled=True)  25.2 us
    psum x1, blocking collectives, local(): route_grad = lax.psum(partial_dot, 'dp')  25.1 us
    all_gather x1, waiting for transfers between devices, local(): preact_grad_all = lax.all_gather(preact_grad, 'dp', axis=0, tiled=True)  24.6 us
    all_to_all x1, starting transfers between devices, local(): lax.all_to_all(out_slice.reshape(block_shape), 'expert', split_axis=1, co...  10.2 us
    all_to_all x1, waiting for transfers between devices, local(): lax.all_to_all(out_slice.reshape(block_shape), 'expert', split_axis=1, co...  7.75 us
  transfers between devices with their start and end apart: 6, of which 5 were waited for; matrix products, arithmetic and copies ran while one was open for 11% of the time, Pallas kernels for 0%

profile of v1, /device:TPU:2, one launch (start us, length us, event | category | flops | bytes accessed | tf_op | source)
XLA Modules:
  0.0 328.0 jit_solution(7390370070552433415)
XLA Ops:
  7.2 0.0 copy-start
  7.2 0.0 reduce-scatter.3.cloned.1.call-start
  7.2 0.9 copy.52
  8.2 0.1 reshape.107
  8.3 0.0 copy-start.3
  8.3 0.6 fusion.7
  8.9 0.8 copy.51
  9.7 0.1 mul.75
  9.8 0.1 convert_element_type.76
  9.9 0.1 fusion.17
  9.9 3.2 fusion.1
  13.1 0.8 select_reduce_fusion
  13.9 1.5 convolution_convert_fusion.1
  15.5 0.0 copy-done.3
  15.5 0.6 fusion.4
  16.1 0.3 pad_maximum_fusion
  16.4 0.5 copy.68
  16.9 84.4 %all_to_all.15 = bf16[2,2,32,24,512]{4,3,1,0,2:T(8,128)(2,1)S(1)} all-to-all(bf16[2,2,32,24,512]{4,3,1,0,2:T(8,128)(2,1)S(1)} %copy.68), channel_id=1, replica_groups=mesh['dp'=8,'expert'=32] {'expert'}, dimensions={2} | all-to-all | bytes 6291456 | tf_op jit(solution)/shard_map/all_to_all | solution.py:46
  101.3 1.3 fusion.31
  102.7 0.1 copy.59
  102.8 0.0 copy-start.1
  102.8 1.2 copy-done.1
  104.0 0.0 copy-done
  104.0 4.2 %convert_bitcast_fusion = bf16[768,2,1536]{2,0,1:T(8,128)(2,1)} fusion(bf16[2,768,512]{2,1,0:T(8,128)(2,1)S(1)} %bitcast.40, bf16[2,512,1536]{2,1,0:T(8,128)(2,1)S(1)} %copy-done), kind=kOutput, calls=%fused_computation.5 | convolution fusion | flops 2418278400 | bytes 9437184 | tf_op jit(solution)/shard_map/lrk,lkf->rlf/dot_general | solution.py:51
  108.2 0.0 reduce-scatter.3.cloned.1.call-update
  108.2 0.0 reduce-scatter.5.cloned.1.call-start
  108.2 0.0 copy-start.4
  108.3 1.6 copy.62
  109.9 0.0 copy-start.2
  109.9 1.2 copy-done.2
  111.1 0.0 copy-done.4
  111.1 2.8 convert_bitcast_fusion.1
  113.9 0.0 reduce-scatter.5.cloned.1.call-update
  113.9 0.0 all-gather.3.cloned.1.call-start
  114.0 32.9 %reduce-scatter.3.cloned.1.call-done = bf16[96,2,1536]{2,0,1:T(8,128)(2,1)} async-done(((bf16[768,2,1536]{2,0,1:T(8,128)(2,1)}), bf16[96,2,1536]{2,0,1:T(8,128)(2,1)}) %reduce-scatter.3.cloned.1.call-update) | async-done | bytes 589840 | tf_op jit(solution)/shard_map/reduce_scatter | solution.py:50
  146.9 2.2 convert_element_type.81
  149.1 37.1 %reduce-scatter.5.cloned.1.call-done = bf16[96,2,768]{2,0,1:T(8,128)(2,1)} async-done(((bf16[768,2,768]{2,0,1:T(8,128)(2,1)}), bf16[96,2,768]{2,0,1:T(8,128)(2,1)}) %reduce-scatter.5.cloned.1.call-update) | async-done | bytes 294928 | tf_op jit(solution)/shard_map/reduce_scatter | solution.py:84
  186.2 2.6 fusion.10
  188.8 0.0 all-gather.3.cloned.1.call-update
  188.8 0.0 all-gather.5.cloned.1.call-start
  188.9 1.9 pad_maximum_fusion.1
  190.8 0.0 all-gather.5.cloned.1.call-update
  190.8 25.2 %all-gather.3.cloned.1.call-done = bf16[768,2,768]{2,0,1:T(8,128)(2,1)} async-done(((bf16[96,2,768]{2,0,1:T(8,128)(2,1)}), bf16[768,2,768]{2,0,1:T(8,128)(2,1)}) %all-gather.3.cloned.1.call-update) | async-done | bytes 2359312 | tf_op jit(solution)/shard_map/all_gather | solution.py:63
  216.0 3.5 %convolution_convert_fusion.3 = bf16[2,768,512]{2,1,0:T(8,128)(2,1)S(1)} fusion(bf16[768,2,768]{2,0,1:T(8,128)(2,1)} %all-gather.3.cloned.1.call-done, bf16[2,768,512]{2,1,0:T(8,128)(2,1)} %param.10), kind=kOutput, calls=%fused_computation.19 | convolution fusion | flops 1208745984 | bytes 5505024 | tf_op jit(solution)/shard_map/rlf,lfk->lrk/dot_general | solution.py:64
  219.5 1.4 copy.60
  220.9 10.2 %all-to-all-start.1 = ((bf16[2,32,24,512]{3,2,0,1:T(8,128)(2,1)}), bf16[2,32,24,512]{3,2,0,1:T(8,128)(2,1)}, u32[]{:S(2)}, u32[]{:S(2)}) async-start(bf16[2,32,24,512]{3,2,0,1:T(8,128)(2,1)} %copy.60), calls=%async_computation.2 | async-start | bytes 3145728 | tf_op jit(solution)/shard_map/all_to_all | solution.py:68
  231.1 24.6 %all-gather.5.cloned.1.call-done = bf16[768,2,1536]{2,0,1:T(8,128)(2,1)} async-done(((bf16[96,2,1536]{2,0,1:T(8,128)(2,1)}), bf16[768,2,1536]{2,0,1:T(8,128)(2,1)}) %all-gather.5.cloned.1.call-update) | async-done | bytes 4718608 | tf_op jit(solution)/shard_map/all_gather | solution.py:95
  255.7 5.0 %convolution_convert_fusion.4 = bf16[2,768,512]{2,1,0:T(8,128)(2,1)S(1)} fusion(bf16[768,2,1536]{2,0,1:T(8,128)(2,1)} %all-gather.5.cloned.1.call-done, bf16[2,512,1536]{2,1,0:T(8,128)(2,1)S(1)} %copy-done), kind=kOutput, calls=%fused_computation.20 | convolution fusion | flops 2416705536 | bytes 9437184 | tf_op jit(solution)/shard_map/rlf,lkf->lrk/dot_general | solution.py:96
  260.6 1.5 copy.63
  262.1 7.7 %all-to-all-done.1 = bf16[2,32,24,512]{3,2,0,1:T(8,128)(2,1)} async-done(((bf16[2,32,24,512]{3,2,0,1:T(8,128)(2,1)}), bf16[2,32,24,512]{3,2,0,1:T(8,128)(2,1)}, u32[]{:S(2)}, u32[]{:S(2)}) %all-to-all-start.1) | async-done | bytes 1572896 | tf_op jit(solution)/shard_map/all_to_all | solution.py:68
  269.9 6.6 %all-to-all-start.2 = ((bf16[2,32,24,512]{3,2,0,1:T(8,128)(2,1)}), bf16[2,32,24,512]{3,2,0,1:T(8,128)(2,1)}, u32[]{:S(2)}, u32[]{:S(2)}) async-start(bf16[2,32,24,512]{3,2,0,1:T(8,128)(2,1)} %copy.63), calls=%async_computation.4 | async-start | bytes 3145728 | tf_op jit(solution)/shard_map/all_to_all | solution.py:105
  276.5 4.7 %convolution_convert_fusion.2 = bf16[2,768,512]{2,1,0:T(8,128)(2,1)} fusion(bf16[768,2,768]{2,0,1:T(8,128)(2,1)} %all-gather.3.cloned.1.call-done, bf16[2,768,512]{2,1,0:T(8,128)(2,1)} %bitcast.43), kind=kOutput, calls=%fused_computation.18 | convolution fusion | flops 1208745984 | bytes 5505024 | tf_op jit(solution)/shard_map/rlf,lrk->lfk/dot_general | solution.py:102
  281.2 1.5 copy.61
  282.7 2.9 bitcast_reduce_fusion
  285.6 0.3 fusion.5
  285.8 0.1 reshape.113
  285.9 25.1 %psum.7 = f32[128,8]{1,0:T(8,128)S(1)} all-reduce(f32[128,8]{1,0:T(8,128)S(1)} %reshape.113), channel_id=1, replica_groups=mesh['dp'=8,'expert'=32] {'dp'}, use_global_device_ids=true, to_apply=%region_7.8 | all-reduce | flops 1024 | bytes 8192 | tf_op jit(solution)/shard_map/psum | solution.py:82
  311.1 0.7 copy.66
  311.7 7.1 %convolution_convert_fusion = bf16[2,512,1536]{2,1,0:T(8,128)(2,1)} fusion(bf16[2,768,512]{2,1,0:T(8,128)(2,1)} %bitcast.41, bf16[768,2,1536]{2,0,1:T(8,128)(2,1)} %all-gather.5.cloned.1.call-done), kind=kOutput, calls=%fused_computation.8 | convolution fusion | flops 2417491968 | bytes 9437184 | tf_op jit(solution)/shard_map/lrk,rlf->lkf/dot_general | solution.py:99
  318.9 0.0 all-to-all-done.2
  318.9 1.5 copy.64
  320.4 1.0 convolution_convert_fusion.5
  (3 shorter events, 0.0 us)
Async XLA Ops:
  7.2 96.8 %copy-start = (bf16[2,512,1536]{2,1,0:T(8,128)(2,1)S(1)}, bf16[2,512,1536]{2,1,0:T(8,128)(2,1)}, u32[]{:S(2)}) copy-start(bf16[2,512,1536]{2,1,0:T(8,128)(2,1)} %param.9) | copy-start | bytes 9437188
  7.2 139.7 %reduce-scatter.3.cloned.1.call-start = ((), (), s32[]{:S(2)}) async-start(), calls=%async_computation.5 | async-start | bytes 5308416 | tf_op jit(solution)/shard_map/reduce_scatter | solution.py:50
  8.3 7.2 %copy-start.3 = (bf16[128,512]{1,0:T(8,128)(2,1)S(1)}, bf16[128,512]{1,0:T(8,128)(2,1)}, u32[]{:S(2)}) copy-start(bf16[128,512]{1,0:T(8,128)(2,1)} %param.11) | copy-start | bytes 393220
  102.8 1.2 copy-start.1
  108.2 78.0 %reduce-scatter.5.cloned.1.call-start = ((), (), s32[]{:S(2)}) async-start(), calls=%async_computation.7 | async-start | bytes 2654208 | tf_op jit(solution)/shard_map/reduce_scatter | solution.py:84
  108.2 2.9 copy-start.4
  109.9 1.2 copy-start.2
  113.9 102.1 %all-gather.3.cloned.1.call-start = ((), (), s32[]{:S(2)}) async-start(), calls=%async_computation.6 | async-start | bytes 2654208 | tf_op jit(solution)/shard_map/all_gather | solution.py:63
  188.8 66.8 %all-gather.5.cloned.1.call-start = ((), (), s32[]{:S(2)}) async-start(), calls=%async_computation.8 | async-start | bytes 5308416 | tf_op jit(solution)/shard_map/all_gather | solution.py:95
  220.9 49.0 %all-to-all-start.1 = ((bf16[2,32,24,512]{3,2,0,1:T(8,128)(2,1)}), bf16[2,32,24,512]{3,2,0,1:T(8,128)(2,1)}, u32[]{:S(2)}, u32[]{:S(2)}) async-start(bf16[2,32,24,512]{3,2,0,1:T(8,128)(2,1)} %copy.60), calls=%async_computation.2 | async-start | bytes 3145728 | tf_op jit(solution)/shard_map/all_to_all | solution.py:68
  269.9 49.0 %all-to-all-start.2 = ((bf16[2,32,24,512]{3,2,0,1:T(8,128)(2,1)}), bf16[2,32,24,512]{3,2,0,1:T(8,128)(2,1)}, u32[]{:S(2)}, u32[]{:S(2)}) async-start(bf16[2,32,24,512]{3,2,0,1:T(8,128)(2,1)} %copy.63), calls=%async_computation.4 | async-start | bytes 3145728 | tf_op jit(solution)/shard_map/all_to_all | solution.py:105
Sparse Core Ops, SparseCore 0:
  108.3 38.4 reduce-scatter.2
  150.0 36.1 reduce-scatter.4
  189.0 26.9 all-gather.2
  218.3 37.3 all-gather.4

commit v2 on v1

--- a/solution.py
+++ b/solution.py
@@ -46,21 +46,32 @@
     both = lax.all_to_all(both, "expert", split_axis=2, concat_axis=2, tiled=True)
     arrived = both[0].reshape(local_count, rows_all, piece_width)
     grad_arrived = both[1].reshape(local_count, rows_all, piece_width)
-    rows = arrived
-    preact = lax.psum_scatter(
-        jnp.einsum("lrk,lkf->rlf", rows, gate_up_weight, preferred_element_type=jnp.float32).astype(
-            jnp.bfloat16
-        ),
+    gate_up_part = jnp.einsum(
+        "lrk,lkf->rlf", arrived, gate_up_weight, preferred_element_type=jnp.float32
+    ).astype(jnp.bfloat16)
+    hidden_grad_part = jnp.einsum(
+        "lrk,lfk->rlf", grad_arrived, down_weight, preferred_element_type=jnp.float32
+    ).astype(jnp.bfloat16)
+    summed = lax.psum_scatter(
+        jnp.concatenate([gate_up_part, hidden_grad_part], axis=2),
         "dp",
         scatter_dimension=0,
         tiled=True,
     ).astype(jnp.float32)
-    gate_pre = preact[..., :hidden_units]
-    up_pre = preact[..., hidden_units:]
+    gate_pre = summed[..., :hidden_units]
+    up_pre = summed[..., hidden_units : 2 * hidden_units]
+    hidden_grad = summed[..., 2 * hidden_units :]
     sigmoid_gate = jax.nn.sigmoid(gate_pre)
     activation = gate_pre * sigmoid_gate
     hidden_mine = (activation * up_pre).astype(jnp.bfloat16)
-    hidden_all = lax.all_gather(hidden_mine, "dp", axis=0, tiled=True)
+    gate_grad = hidden_grad * up_pre * sigmoid_gate * (1.0 + gate_pre * (1.0 - sigmoid_gate))
+    up_grad = hidden_grad * activation
+    preact_grad = jnp.concatenate([gate_grad, up_grad], axis=2).astype(jnp.bfloat16)
+    gathered = lax.all_gather(
+        jnp.concatenate([hidden_mine, preact_grad], axis=2), "dp", axis=0, tiled=True
+    )
+    hidden_all = gathered[..., :hidden_units]
+    preact_grad_all = gathered[..., hidden_units:]
     out_slice = jnp.einsum(
         "rlf,lfk->lrk", hidden_all, down_weight, preferred_element_type=jnp.float32
     ).astype(jnp.bfloat16)
@@ -80,19 +91,6 @@
     )
     partial_dot = jnp.sum(grad_routes * y_routes, axis=1).reshape(tok_count, top_count)
     route_grad = lax.psum(partial_dot, "dp")
-    rows = grad_arrived
-    hidden_grad = lax.psum_scatter(
-        jnp.einsum("lrk,lfk->rlf", rows, down_weight, preferred_element_type=jnp.float32).astype(
-            jnp.bfloat16
-        ),
-        "dp",
-        scatter_dimension=0,
-        tiled=True,
-    ).astype(jnp.float32)
-    gate_grad = hidden_grad * up_pre * sigmoid_gate * (1.0 + gate_pre * (1.0 - sigmoid_gate))
-    up_grad = hidden_grad * activation
-    preact_grad = jnp.concatenate([gate_grad, up_grad], axis=2).astype(jnp.bfloat16)
-    preact_grad_all = lax.all_gather(preact_grad, "dp", axis=0, tiled=True)
     x_grad_slice = jnp.einsum(
         "rlf,lkf->lrk", preact_grad_all, gate_up_weight, preferred_element_type=jnp.float32
     ).astype(jnp.bfloat16)

time: 329 us -> 323 us (0.982)
  local copies, waits for them, and re-layouts: 14.6 us -> 9.41 us
    all_to_all x1, waiting for transfers between devices: 7.75 us -> 32.5 us  [local(): lax.all_to_all(out_slice.reshape(block_shape), 'expert', split_axis=1, co...]
    reduce_scatter x2 -> x1, waiting for transfers between devices: 70 us -> 45.8 us  [local(): lax.psum_scatter(jnp.concatenate([gate_up_part, hidden_grad_part], axis=2...]
    concatenate x1 -> x2, other arithmetic: 1.91 us -> 7.4 us  [the longest x1 6.43 us: local(): jnp.concatenate([gate_up_part, hidden_grad_part], axis=2)]
    all_gather x2 -> x1, waiting for transfers between devices: 49.8 us -> 46.5 us  [local(): lax.all_gather(jnp.concatenate([hidden_mine, preact_grad], axis=2), 'dp',...]
  transfers between devices with their start and end apart: 6 -> 4, of which waited for: 5 -> 3; matrix products, arithmetic and copies ran while one was open for 11% -> 7% of each run, Pallas kernels for 0% -> 0%
where the time goes in v2:
time: 323 us; the launch traced here: 322 us
  waiting for transfers between devices  125 us (39%)
  blocking collectives  110 us (34%)
  matrix products  33.4 us (10%)
  starting transfers between devices  16.9 us (5%)
  between operations  14.3 us (4%)
  other arithmetic  13.6 us (4%)
  local copies, waits for them, and re-layouts  9.41 us (3%)
    all_to_all x1, blocking collectives, local(): lax.all_to_all(both, 'expert', split_axis=2, concat_axis=2, tiled=True)  84.4 us
    all_gather x1, waiting for transfers between devices, local(): lax.all_gather(jnp.concatenate([hidden_mine, preact_grad], axis=2), 'dp',...  46.5 us
    reduce_scatter x1, waiting for transfers between devices, local(): lax.psum_scatter(jnp.concatenate([gate_up_part, hidden_grad_part], axis=2...  45.8 us
    all_to_all x1, waiting for transfers between devices, local(): lax.all_to_all(out_slice.reshape(block_shape), 'expert', split_axis=1, co...  32.5 us
    psum x1, blocking collectives, local(): route_grad = lax.psum(partial_dot, 'dp')  25.1 us
    all_to_all x1, starting transfers between devices, local(): lax.all_to_all(out_slice.reshape(block_shape), 'expert', split_axis=1, co...  10.2 us
    all_to_all x1, starting transfers between devices, local(): lax.all_to_all(x_grad_slice.reshape(block_shape), 'expert', split_axis=1,...  6.56 us
  transfers between devices with their start and end apart: 4, of which 3 were waited for; matrix products, arithmetic and copies ran while one was open for 7% of the time, Pallas kernels for 0%

profile of v2, /device:TPU:2, one launch (start us, length us, event | category | flops | bytes accessed | tf_op | source)
XLA Modules:
  0.0 322.0 jit_solution(14273040128306517950)
XLA Ops:
  7.2 0.0 copy-start
  7.2 0.0 copy-start.4
  7.2 0.0 reduce-scatter.2.cloned.1.call-start
  7.2 0.9 copy.60
  8.2 0.1 reshape.107
  8.3 0.6 fusion.27
  8.9 0.8 copy.59
  9.7 0.1 mul.75
  9.8 0.1 convert_element_type.73
  9.9 0.1 fusion.33
  10.0 3.2 fusion.1
  13.1 0.8 select_reduce_fusion
  13.9 1.5 convolution_convert_fusion
  15.5 0.0 copy-done.4
  15.5 0.6 fusion.11
  16.1 0.3 pad_maximum_fusion.1
  16.4 0.5 copy.80
  16.9 84.4 %all_to_all.15 = bf16[2,2,32,24,512]{4,3,1,0,2:T(8,128)(2,1)S(1)} all-to-all(bf16[2,2,32,24,512]{4,3,1,0,2:T(8,128)(2,1)S(1)} %copy.80), channel_id=1, replica_groups=mesh['dp'=8,'expert'=32] {'expert'}, dimensions={2} | all-to-all | bytes 6291456 | tf_op jit(solution)/shard_map/all_to_all | solution.py:46
  101.3 0.2 fusion.47
  101.6 0.1 copy.67
  101.7 0.0 copy-start.1
  101.7 0.1 copy.68
  101.8 0.0 copy-start.3
  101.8 0.0 copy-done
  101.9 0.0 copy-start.5
  101.9 4.2 %convert_bitcast_fusion = bf16[768,2,1536]{2,0,1:T(8,128)(2,1)} fusion(bf16[2,768,512]{2,1,0:T(8,128)(2,1)S(1)} %bitcast.36, bf16[2,512,1536]{2,1,0:T(8,128)(2,1)S(1)} %copy-done), kind=kOutput, calls=%fused_computation.6 | convolution fusion | flops 2418278400 | bytes 9437184 | tf_op jit(solution)/shard_map/lrk,lkf->rlf/dot_general | solution.py:49
  106.1 0.0 copy-done.1
  106.1 0.0 copy-done.3
  106.1 0.0 copy-done.5
  106.1 2.8 convert_bitcast_fusion.1
  108.9 6.4 %pad_maximum_fusion = bf16[768,2,2304]{2,0,1:T(8,128)(2,1)} fusion(bf16[768,2,768]{2,0,1:T(8,128)(2,1)} %convert_bitcast_fusion.1, bf16[768,2,1536]{2,0,1:T(8,128)(2,1)} %convert_bitcast_fusion), kind=kLoop, calls=%fused_computation | loop fusion | flops 14155776 | bytes 14155776 | tf_op jit(solution)/shard_map/concatenate | solution.py:56
  115.3 0.0 reduce-scatter.2.cloned.1.call-update
  115.4 0.0 all-gather.2.cloned.1.call-start
  115.4 45.8 %reduce-scatter.2.cloned.1.call-done = bf16[96,2,2304]{2,0,1:T(8,128)(2,1)} async-done(((bf16[768,2,2304]{2,0,1:T(8,128)(2,1)}), bf16[96,2,2304]{2,0,1:T(8,128)(2,1)}) %reduce-scatter.2.cloned.1.call-update) | async-done | bytes 884752 | tf_op jit(solution)/shard_map/reduce_scatter | solution.py:55
  161.2 1.3 convert_element_type.80
  162.5 0.3 multiply_convert_fusion.2
  162.8 1.0 pad_maximum_fusion.2
  163.8 0.0 all-gather.2.cloned.1.call-update
  163.8 46.5 %all-gather.2.cloned.1.call-done = bf16[768,2,2304]{2,0,1:T(8,128)(2,1)} async-done(((bf16[96,2,2304]{2,0,1:T(8,128)(2,1)}), bf16[768,2,2304]{2,0,1:T(8,128)(2,1)}) %all-gather.2.cloned.1.call-update) | async-done | bytes 7077904 | tf_op jit(solution)/shard_map/all_gather | solution.py:70
  210.3 3.5 %fusion.17 = bf16[2,768,512]{2,1,0:T(8,128)(2,1)S(1)} fusion(bf16[2,768,512]{2,1,0:T(8,128)(2,1)} %param.10, bf16[768,2,2304]{2,0,1:T(8,128)(2,1)} %all-gather.2.cloned.1.call-done), kind=kOutput, calls=%fused_computation.27 | convolution fusion | flops 1208745984 | bytes 5505024 | tf_op jit(solution)/shard_map/rlf,lfk->lrk/dot_general | solution.py:75
  213.9 1.3 copy.70
  215.2 10.2 %all-to-all-start.1 = ((bf16[2,32,24,512]{3,2,0,1:T(8,128)(2,1)}), bf16[2,32,24,512]{3,2,0,1:T(8,128)(2,1)}, u32[]{:S(2)}, u32[]{:S(2)}) async-start(bf16[2,32,24,512]{3,2,0,1:T(8,128)(2,1)} %copy.70), calls=%async_computation.2 | async-start | bytes 3145728 | tf_op jit(solution)/shard_map/all_to_all | solution.py:79
  225.4 5.0 %fusion.23 = bf16[2,768,512]{2,1,0:T(8,128)(2,1)S(1)} fusion(bf16[2,512,1536]{2,1,0:T(8,128)(2,1)S(1)} %copy-done, bf16[768,2,2304]{2,0,1:T(8,128)(2,1)} %all-gather.2.cloned.1.call-done), kind=kOutput, calls=%fused_computation.29 | convolution fusion | flops 2416705536 | bytes 9437184 | tf_op jit(solution)/shard_map/rlf,lkf->lrk/dot_general | solution.py:94
  230.4 1.3 copy.72
  231.7 32.5 %all-to-all-done.1 = bf16[2,32,24,512]{3,2,0,1:T(8,128)(2,1)} async-done(((bf16[2,32,24,512]{3,2,0,1:T(8,128)(2,1)}), bf16[2,32,24,512]{3,2,0,1:T(8,128)(2,1)}, u32[]{:S(2)}, u32[]{:S(2)}) %all-to-all-start.1) | async-done | bytes 1572896 | tf_op jit(solution)/shard_map/all_to_all | solution.py:79
  264.2 6.6 %all-to-all-start.2 = ((bf16[2,32,24,512]{3,2,0,1:T(8,128)(2,1)}), bf16[2,32,24,512]{3,2,0,1:T(8,128)(2,1)}, u32[]{:S(2)}, u32[]{:S(2)}) async-start(bf16[2,32,24,512]{3,2,0,1:T(8,128)(2,1)} %copy.72), calls=%async_computation.3 | async-start | bytes 3145728 | tf_op jit(solution)/shard_map/all_to_all | solution.py:103
  270.8 0.0 copy-start.2
  270.8 4.8 %fusion.20 = bf16[2,768,512]{2,1,0:T(8,128)(2,1)} fusion(bf16[2,768,512]{2,1,0:T(8,128)(2,1)} %bitcast.39, bf16[768,2,2304]{2,0,1:T(8,128)(2,1)} %all-gather.2.cloned.1.call-done), kind=kOutput, calls=%fused_computation.28 | convolution fusion | flops 1208745984 | bytes 5505024 | tf_op jit(solution)/shard_map/rlf,lrk->lfk/dot_general | solution.py:100
  275.6 0.0 copy-done.2
  275.6 6.4 %fusion.7 = bf16[2,512,1536]{2,1,0:T(8,128)(2,1)} fusion(bf16[2,768,512]{2,1,0:T(8,128)(2,1)S(1)} %bitcast.37, bf16[768,2,2304]{2,0,1:T(8,128)(2,1)} %all-gather.2.cloned.1.call-done), kind=kOutput, calls=%fused_computation.13 | convolution fusion | flops 2417491968 | bytes 9437184 | tf_op jit(solution)/shard_map/lrk,rlf->lkf/dot_general | solution.py:97
  282.0 1.5 copy.71
  283.5 2.9 bitcast_reduce_fusion
  286.4 0.3 fusion.12
  286.7 0.1 reshape.113
  286.8 25.1 %psum.7 = f32[128,8]{1,0:T(8,128)S(1)} all-reduce(f32[128,8]{1,0:T(8,128)S(1)} %reshape.113), channel_id=1, replica_groups=mesh['dp'=8,'expert'=32] {'dp'}, use_global_device_ids=true, to_apply=%region_6.7 | all-reduce | flops 1024 | bytes 8192 | tf_op jit(solution)/shard_map/psum | solution.py:93
  311.9 0.7 copy.76
  312.6 0.0 all-to-all-done.2
  312.6 1.5 copy.73
  314.1 1.0 convolution_convert_fusion.1
  (3 shorter events, 0.0 us)
Async XLA Ops:
  7.2 94.7 %copy-start = (bf16[2,512,1536]{2,1,0:T(8,128)(2,1)S(1)}, bf16[2,512,1536]{2,1,0:T(8,128)(2,1)}, u32[]{:S(2)}) copy-start(bf16[2,512,1536]{2,1,0:T(8,128)(2,1)} %param.9) | copy-start | bytes 9437188
  7.2 8.3 %copy-start.4 = (bf16[128,512]{1,0:T(8,128)(2,1)S(1)}, bf16[128,512]{1,0:T(8,128)(2,1)}, u32[]{:S(2)}) copy-start(bf16[128,512]{1,0:T(8,128)(2,1)} %param.11) | copy-start | bytes 393220
  7.2 154.0 %reduce-scatter.2.cloned.1.call-start = ((), (), s32[]{:S(2)}) async-start(), calls=%async_computation.4 | async-start | bytes 7962624 | tf_op jit(solution)/shard_map/reduce_scatter | solution.py:55
  101.7 4.4 %copy-start.1 = (bf16[1,2,32,24,512]{4,3,2,1,0:T(8,128)(2,1)}, bf16[1,2,32,24,512]{4,3,2,1,0:T(8,128)(2,1)S(1)}, u32[]{:S(2)}) copy-start(bf16[1,2,32,24,512]{4,3,2,1,0:T(8,128)(2,1)S(1)} %copy.67) | copy-start | bytes 4718596
  101.8 4.2 %copy-start.3 = (bf16[1,2,32,24,512]{4,3,2,1,0:T(8,128)(2,1)}, bf16[1,2,32,24,512]{4,3,2,1,0:T(8,128)(2,1)S(1)}, u32[]{:S(2)}) copy-start(bf16[1,2,32,24,512]{4,3,2,1,0:T(8,128)(2,1)S(1)} %copy.68) | copy-start | bytes 4718596
  101.9 4.2 %copy-start.5 = (bf16[2,768,512]{2,1,0:T(8,128)(2,1)S(1)}, bf16[2,768,512]{2,1,0:T(8,128)(2,1)}, u32[]{:S(2)}) copy-start(bf16[2,768,512]{2,1,0:T(8,128)(2,1)} %param.10) | copy-start | bytes 4718596
  115.4 95.0 %all-gather.2.cloned.1.call-start = ((), (), s32[]{:S(2)}) async-start(), calls=%async_computation.5 | async-start | bytes 7962624 | tf_op jit(solution)/shard_map/all_gather | solution.py:70
  215.2 49.0 %all-to-all-start.1 = ((bf16[2,32,24,512]{3,2,0,1:T(8,128)(2,1)}), bf16[2,32,24,512]{3,2,0,1:T(8,128)(2,1)}, u32[]{:S(2)}, u32[]{:S(2)}) async-start(bf16[2,32,24,512]{3,2,0,1:T(8,128)(2,1)} %copy.70), calls=%async_computation.2 | async-start | bytes 3145728 | tf_op jit(solution)/shard_map/all_to_all | solution.py:79
  264.2 48.4 %all-to-all-start.2 = ((bf16[2,32,24,512]{3,2,0,1:T(8,128)(2,1)}), bf16[2,32,24,512]{3,2,0,1:T(8,128)(2,1)}, u32[]{:S(2)}, u32[]{:S(2)}) async-start(bf16[2,32,24,512]{3,2,0,1:T(8,128)(2,1)} %copy.72), calls=%async_computation.3 | async-start | bytes 3145728 | tf_op jit(solution)/shard_map/all_to_all | solution.py:103
  270.8 4.8 %copy-start.2 = (bf16[1,2,32,24,512]{4,3,2,1,0:T(8,128)(2,1)S(1)}, bf16[1,2,32,24,512]{4,3,2,1,0:T(8,128)(2,1)}, u32[]{:S(2)}) copy-start(bf16[1,2,32,24,512]{4,3,2,1,0:T(8,128)(2,1)} %copy-done.1) | copy-start | bytes 4718596
Sparse Core Ops, SparseCore 0:
  115.5 45.7 reduce-scatter.1
  164.0 46.3 all-gather.1

commit v3 on v2

--- a/solution.py
+++ b/solution.py
@@ -67,11 +67,8 @@
     gate_grad = hidden_grad * up_pre * sigmoid_gate * (1.0 + gate_pre * (1.0 - sigmoid_gate))
     up_grad = hidden_grad * activation
     preact_grad = jnp.concatenate([gate_grad, up_grad], axis=2).astype(jnp.bfloat16)
-    gathered = lax.all_gather(
-        jnp.concatenate([hidden_mine, preact_grad], axis=2), "dp", axis=0, tiled=True
-    )
-    hidden_all = gathered[..., :hidden_units]
-    preact_grad_all = gathered[..., hidden_units:]
+    hidden_all = lax.all_gather(hidden_mine, "dp", axis=0, tiled=True)
+    preact_grad_all = lax.all_gather(preact_grad, "dp", axis=0, tiled=True)
     out_slice = jnp.einsum(
         "rlf,lfk->lrk", hidden_all, down_weight, preferred_element_type=jnp.float32
     ).astype(jnp.bfloat16)

time: 323 us -> 304 us (0.941)
  waiting for transfers between devices: 125 us -> 104 us
    all_to_all x1, waiting for transfers between devices: 32.5 us -> 7.63 us  [local(): lax.all_to_all(out_slice.reshape(block_shape), 'expert', split_axis=1, co...]
    all_gather x1 -> x2, waiting for transfers between devices: 46.5 us -> 50.7 us  [the longest x1 25.9 us: local(): hidden_all = lax.all_gather(hidden_mine, 'dp', axis=0, tiled=True)]
  transfers between devices with their start and end apart: 4 -> 5, of which waited for: 3 -> 4; matrix products, arithmetic and copies ran while one was open for 7% -> 10% of each run, Pallas kernels for 0% -> 0%
where the time goes in v3:
time: 304 us
  blocking collectives  110 us (36%)
  waiting for transfers between devices  104 us (34%)
  matrix products  34 us (11%)
  starting transfers between devices  16.9 us (6%)
  other arithmetic  15.4 us (5%)
  between operations  14 us (5%)
  local copies, waits for them, and re-layouts  9.53 us (3%)
    all_to_all x1, blocking collectives, local(): lax.all_to_all(both, 'expert', split_axis=2, concat_axis=2, tiled=True)  84.4 us
    reduce_scatter x1, waiting for transfers between devices, local(): lax.psum_scatter(jnp.concatenate([gate_up_part, hidden_grad_part], axis=2...  45.8 us
    all_gather x1, waiting for transfers between devices, local(): hidden_all = lax.all_gather(hidden_mine, 'dp', axis=0, tiled=True)  25.9 us
    psum x1, blocking collectives, local(): route_grad = lax.psum(partial_dot, 'dp')  25.1 us
    all_gather x1, waiting for transfers between devices, local(): preact_grad_all = lax.all_gather(preact_grad, 'dp', axis=0, tiled=True)  24.8 us
    all_to_all x1, starting transfers between devices, local(): lax.all_to_all(out_slice.reshape(block_shape), 'expert', split_axis=1, co...  10.2 us
    all_to_all x1, waiting for transfers between devices, local(): lax.all_to_all(out_slice.reshape(block_shape), 'expert', split_axis=1, co...  7.63 us
    dot_general x1, matrix products, local(): jnp.einsum('lrk,rlf->lkf', arrived, preact_grad_all, preferred_element_ty...  7.13 us
  transfers between devices with their start and end apart: 5, of which 4 were waited for; matrix products, arithmetic and copies ran while one was open for 10% of the time, Pallas kernels for 0%

profile of v3, /device:TPU:2, one launch (start us, length us, event | category | flops | bytes accessed | tf_op | source)
XLA Modules:
  0.0 303.6 jit_solution(3204589052721626172)
XLA Ops:
  7.2 0.0 copy-start
  7.2 0.0 reduce-scatter.2.cloned.1.call-start
  7.2 0.9 copy.56
  8.2 0.1 reshape.107
  8.3 0.0 copy-start.3
  8.3 0.6 fusion.7
  8.9 0.8 copy.55
  9.7 0.1 mul.75
  9.8 0.1 convert_element_type.73
  9.9 0.1 fusion.13
  9.9 3.2 %fusion.1 = pred[128,1536]{1,0:T(8,128)(4,1)S(1)} fusion(s32[128,8]{1,0:T(8,128)S(1)} %fusion.13), kind=kLoop, calls=%fused_computation.5 | loop fusion | flops 2949120 | bytes 200704 | tf_op jit(solution)/shard_map/reduce_or | solution.py:31
  13.1 0.8 select_reduce_fusion
  13.9 1.5 convolution_convert_fusion.1
  15.5 0.0 copy-done.3
  15.5 0.6 fusion.4
  16.1 0.3 pad_maximum_fusion.1
  16.4 0.5 copy.74
  16.9 84.4 %all_to_all.15 = bf16[2,2,32,24,512]{4,3,1,0,2:T(8,128)(2,1)S(1)} all-to-all(bf16[2,2,32,24,512]{4,3,1,0,2:T(8,128)(2,1)S(1)} %copy.74), channel_id=1, replica_groups=mesh['dp'=8,'expert'=32] {'expert'}, dimensions={2} | all-to-all | bytes 6291456 | tf_op jit(solution)/shard_map/all_to_all | solution.py:46
  101.3 0.2 fusion.27
  101.6 0.1 copy.63
  101.7 0.0 copy-start.1
  101.7 0.1 copy.64
  101.8 0.0 copy-start.2
  101.8 0.0 copy-done
  101.8 0.0 copy-start.4
  101.9 4.2 %convert_bitcast_fusion = bf16[768,2,1536]{2,0,1:T(8,128)(2,1)} fusion(bf16[2,768,512]{2,1,0:T(8,128)(2,1)S(1)} %bitcast.40, bf16[2,512,1536]{2,1,0:T(8,128)(2,1)S(1)} %copy-done), kind=kOutput, calls=%fused_computation.6 | convolution fusion | flops 2418278400 | bytes 9437184 | tf_op jit(solution)/shard_map/lrk,lkf->rlf/dot_general | solution.py:49
  106.1 0.0 copy-done.1
  106.1 0.0 copy-done.2
  106.1 0.0 copy-done.4
  106.1 2.8 convert_bitcast_fusion.1
  108.9 6.4 %pad_maximum_fusion = bf16[768,2,2304]{2,0,1:T(8,128)(2,1)} fusion(bf16[768,2,768]{2,0,1:T(8,128)(2,1)} %convert_bitcast_fusion.1, bf16[768,2,1536]{2,0,1:T(8,128)(2,1)} %convert_bitcast_fusion), kind=kLoop, calls=%fused_computation | loop fusion | flops 14155776 | bytes 14155776 | tf_op jit(solution)/shard_map/concatenate | solution.py:56
  115.3 0.0 reduce-scatter.2.cloned.1.call-update
  115.3 0.0 all-gather.3.cloned.1.call-start
  115.4 45.8 %reduce-scatter.2.cloned.1.call-done = bf16[96,2,2304]{2,0,1:T(8,128)(2,1)} async-done(((bf16[768,2,2304]{2,0,1:T(8,128)(2,1)}), bf16[96,2,2304]{2,0,1:T(8,128)(2,1)}) %reduce-scatter.2.cloned.1.call-update) | async-done | bytes 884752 | tf_op jit(solution)/shard_map/reduce_scatter | solution.py:55
  161.2 1.3 convert_element_type.80
  162.5 1.2 multiply_convert_fusion.1
  163.7 0.0 all-gather.3.cloned.1.call-update
  163.7 0.0 all-gather.5.cloned.1.call-start
  163.7 1.9 pad_maximum_fusion.2
  165.6 0.0 all-gather.5.cloned.1.call-update
  165.7 25.9 %all-gather.3.cloned.1.call-done = bf16[768,2,768]{2,0,1:T(8,128)(2,1)} async-done(((bf16[96,2,768]{2,0,1:T(8,128)(2,1)}), bf16[768,2,768]{2,0,1:T(8,128)(2,1)}) %all-gather.3.cloned.1.call-update) | async-done | bytes 2359312 | tf_op jit(solution)/shard_map/all_gather | solution.py:70
  191.6 3.5 %convolution_convert_fusion.3 = bf16[2,768,512]{2,1,0:T(8,128)(2,1)S(1)} fusion(bf16[768,2,768]{2,0,1:T(8,128)(2,1)} %all-gather.3.cloned.1.call-done, bf16[2,768,512]{2,1,0:T(8,128)(2,1)} %param.10), kind=kOutput, calls=%fused_computation.20 | convolution fusion | flops 1208745984 | bytes 5505024 | tf_op jit(solution)/shard_map/rlf,lfk->lrk/dot_general | solution.py:72
  195.1 1.4 copy.66
  196.5 10.2 %all-to-all-start.1 = ((bf16[2,32,24,512]{3,2,0,1:T(8,128)(2,1)}), bf16[2,32,24,512]{3,2,0,1:T(8,128)(2,1)}, u32[]{:S(2)}, u32[]{:S(2)}) async-start(bf16[2,32,24,512]{3,2,0,1:T(8,128)(2,1)} %copy.66), calls=%async_computation.2 | async-start | bytes 3145728 | tf_op jit(solution)/shard_map/all_to_all | solution.py:76
  206.7 24.8 %all-gather.5.cloned.1.call-done = bf16[768,2,1536]{2,0,1:T(8,128)(2,1)} async-done(((bf16[96,2,1536]{2,0,1:T(8,128)(2,1)}), bf16[768,2,1536]{2,0,1:T(8,128)(2,1)}) %all-gather.5.cloned.1.call-update) | async-done | bytes 4718608 | tf_op jit(solution)/shard_map/all_gather | solution.py:71
  231.4 5.0 %convolution_convert_fusion.4 = bf16[2,768,512]{2,1,0:T(8,128)(2,1)S(1)} fusion(bf16[768,2,1536]{2,0,1:T(8,128)(2,1)} %all-gather.5.cloned.1.call-done, bf16[2,512,1536]{2,1,0:T(8,128)(2,1)S(1)} %copy-done), kind=kOutput, calls=%fused_computation.21 | convolution fusion | flops 2416705536 | bytes 9437184 | tf_op jit(solution)/shard_map/rlf,lkf->lrk/dot_general | solution.py:91
  236.4 1.4 copy.68
  237.8 7.6 %all-to-all-done.1 = bf16[2,32,24,512]{3,2,0,1:T(8,128)(2,1)} async-done(((bf16[2,32,24,512]{3,2,0,1:T(8,128)(2,1)}), bf16[2,32,24,512]{3,2,0,1:T(8,128)(2,1)}, u32[]{:S(2)}, u32[]{:S(2)}) %all-to-all-start.1) | async-done | bytes 1572896 | tf_op jit(solution)/shard_map/all_to_all | solution.py:76
  245.5 6.6 %all-to-all-start.2 = ((bf16[2,32,24,512]{3,2,0,1:T(8,128)(2,1)}), bf16[2,32,24,512]{3,2,0,1:T(8,128)(2,1)}, u32[]{:S(2)}, u32[]{:S(2)}) async-start(bf16[2,32,24,512]{3,2,0,1:T(8,128)(2,1)} %copy.68), calls=%async_computation.3 | async-start | bytes 3145728 | tf_op jit(solution)/shard_map/all_to_all | solution.py:100
  252.1 4.7 %convolution_convert_fusion.2 = bf16[2,768,512]{2,1,0:T(8,128)(2,1)} fusion(bf16[768,2,768]{2,0,1:T(8,128)(2,1)} %all-gather.3.cloned.1.call-done, bf16[2,768,512]{2,1,0:T(8,128)(2,1)} %bitcast.43), kind=kOutput, calls=%fused_computation.19 | convolution fusion | flops 1208745984 | bytes 5505024 | tf_op jit(solution)/shard_map/rlf,lrk->lfk/dot_general | solution.py:97
  256.8 1.5 copy.67
  258.3 2.9 bitcast_reduce_fusion
  261.2 0.3 fusion.5
  261.5 0.1 reshape.113
  261.5 25.1 %psum.7 = f32[128,8]{1,0:T(8,128)S(1)} all-reduce(f32[128,8]{1,0:T(8,128)S(1)} %reshape.113), channel_id=1, replica_groups=mesh['dp'=8,'expert'=32] {'dp'}, use_global_device_ids=true, to_apply=%region_6.7 | all-reduce | flops 1024 | bytes 8192 | tf_op jit(solution)/shard_map/psum | solution.py:90
  286.7 0.7 copy.71
  287.4 7.1 %convolution_convert_fusion = bf16[2,512,1536]{2,1,0:T(8,128)(2,1)} fusion(bf16[2,768,512]{2,1,0:T(8,128)(2,1)} %bitcast.41, bf16[768,2,1536]{2,0,1:T(8,128)(2,1)} %all-gather.5.cloned.1.call-done), kind=kOutput, calls=%fused_computation.9 | convolution fusion | flops 2417491968 | bytes 9437184 | tf_op jit(solution)/shard_map/lrk,rlf->lkf/dot_general | solution.py:94
  294.5 0.0 all-to-all-done.2
  294.5 1.5 copy.69
  296.0 1.0 convolution_convert_fusion.5
  (3 shorter events, 0.0 us)
Async XLA Ops:
  7.2 94.7 %copy-start = (bf16[2,512,1536]{2,1,0:T(8,128)(2,1)S(1)}, bf16[2,512,1536]{2,1,0:T(8,128)(2,1)}, u32[]{:S(2)}) copy-start(bf16[2,512,1536]{2,1,0:T(8,128)(2,1)} %param.9) | copy-start | bytes 9437188
  7.2 154.0 %reduce-scatter.2.cloned.1.call-start = ((), (), s32[]{:S(2)}) async-start(), calls=%async_computation.4 | async-start | bytes 7962624 | tf_op jit(solution)/shard_map/reduce_scatter | solution.py:55
  8.3 7.2 %copy-start.3 = (bf16[128,512]{1,0:T(8,128)(2,1)S(1)}, bf16[128,512]{1,0:T(8,128)(2,1)}, u32[]{:S(2)}) copy-start(bf16[128,512]{1,0:T(8,128)(2,1)} %param.11) | copy-start | bytes 393220
  101.7 4.4 %copy-start.1 = (bf16[1,2,32,24,512]{4,3,2,1,0:T(8,128)(2,1)}, bf16[1,2,32,24,512]{4,3,2,1,0:T(8,128)(2,1)S(1)}, u32[]{:S(2)}) copy-start(bf16[1,2,32,24,512]{4,3,2,1,0:T(8,128)(2,1)S(1)} %copy.63) | copy-start | bytes 4718596
  101.8 4.2 %copy-start.2 = (bf16[1,2,32,24,512]{4,3,2,1,0:T(8,128)(2,1)}, bf16[1,2,32,24,512]{4,3,2,1,0:T(8,128)(2,1)S(1)}, u32[]{:S(2)}) copy-start(bf16[1,2,32,24,512]{4,3,2,1,0:T(8,128)(2,1)S(1)} %copy.64) | copy-start | bytes 4718596
  101.8 4.2 %copy-start.4 = (bf16[2,768,512]{2,1,0:T(8,128)(2,1)S(1)}, bf16[2,768,512]{2,1,0:T(8,128)(2,1)}, u32[]{:S(2)}) copy-start(bf16[2,768,512]{2,1,0:T(8,128)(2,1)} %param.10) | copy-start | bytes 4718596
  115.3 76.3 %all-gather.3.cloned.1.call-start = ((), (), s32[]{:S(2)}) async-start(), calls=%async_computation.5 | async-start | bytes 2654208 | tf_op jit(solution)/shard_map/all_gather | solution.py:70
  163.7 67.8 %all-gather.5.cloned.1.call-start = ((), (), s32[]{:S(2)}) async-start(), calls=%async_computation.6 | async-start | bytes 5308416 | tf_op jit(solution)/shard_map/all_gather | solution.py:71
  196.5 49.0 %all-to-all-start.1 = ((bf16[2,32,24,512]{3,2,0,1:T(8,128)(2,1)}), bf16[2,32,24,512]{3,2,0,1:T(8,128)(2,1)}, u32[]{:S(2)}, u32[]{:S(2)}) async-start(bf16[2,32,24,512]{3,2,0,1:T(8,128)(2,1)} %copy.66), calls=%async_computation.2 | async-start | bytes 3145728 | tf_op jit(solution)/shard_map/all_to_all | solution.py:76
  245.5 49.0 %all-to-all-start.2 = ((bf16[2,32,24,512]{3,2,0,1:T(8,128)(2,1)}), bf16[2,32,24,512]{3,2,0,1:T(8,128)(2,1)}, u32[]{:S(2)}, u32[]{:S(2)}) async-start(bf16[2,32,24,512]{3,2,0,1:T(8,128)(2,1)} %copy.68), calls=%async_computation.3 | async-start | bytes 3145728 | tf_op jit(solution)/shard_map/all_to_all | solution.py:100
Sparse Core Ops, SparseCore 0:
  115.5 45.7 reduce-scatter.1
  163.8 27.7 all-gather.2
  194.0 37.3 all-gather.4
